TPU v7x, 512 devices: a whole 4x4x16 slice. The times are simulated.
512 devices in a mesh: replica: 64 (over z, x), shard: 8 (over y, core).
Axes of the slice: x: 4, y: 4, z: 16, core: 2. Of those that a mesh axis runs over, the one named last changes fastest.
Arguments:
- grad_query: float32 [512, 512, 384], P(('replica', 'shard')), may hold values from -1.25 to 1.25
- grad_output: float32 [512, 384, 512], P(('replica', 'shard')), may hold values from -1.25 to 1.25
- grad_norm: float32 [512, 512], P(('replica', 'shard')), may hold values from -1.25 to 1.25
- grad_bias: float32 [512, 32, 6], P(('replica', 'shard')), may hold values from -0.3 to 0.3
- weight_query: float32 [512, 384], P('shard'), may hold values from -5.303301 to 5.303301
- weight_output: float32 [384, 512], P('shard'), may hold values from -6.1237244 to 6.1237244
- weight_norm: float32 [512], P('shard'), may hold values from 0 to 120
- weight_bias: float32 [32, 6], P('shard'), may hold values from -120 to 120
- first_query: float32 [512, 384], P('shard'), may hold values from -120 to 120
- first_output: float32 [384, 512], P('shard'), may hold values from -120 to 120
- first_norm: float32 [512], P('shard'), may hold values from -120 to 120
- first_bias: float32 [32, 6], P('shard'), may hold values from -120 to 120
- second_query: float32 [512, 384], P('shard'), may hold values from 0.05 to 2
- second_output: float32 [384, 512], P('shard'), may hold values from 0.05 to 2
- second_norm: float32 [512], P('shard'), may hold values from 0.05 to 2
- second_bias: float32 [32, 6], P('shard'), may hold values from 0.05 to 2
Outputs:
- updated_query: bfloat16 [512, 384], replicated
- updated_output: bfloat16 [384, 512], replicated
- updated_norm: bfloat16 [512], replicated
- updated_bias: bfloat16 [32, 6], replicated
- first_query_next: float32 [512, 384], P('shard')
- first_output_next: float32 [384, 512], P('shard')
- first_norm_next: float32 [512], P('shard')
- first_bias_next: float32 [32, 6], P('shard')
- second_query_next: float32 [512, 384], P('shard')
- second_output_next: float32 [384, 512], P('shard')
- second_norm_next: float32 [512], P('shard')
- second_bias_next: float32 [32, 6], P('shard')
- norm_table: float32 [2, 4], replicated
- trust_ratios: float32 [4], replicated
All inputs are finite; a program needn't handle non-finite values.
Results may differ from a plain program's by a relative error of at most 0.008.
Values may be sent and summed in bfloat16 or wider, within the bound.
No kernel may reach another device: no remote copies, remote signals or barrier semaphores. Data moves between devices by JAX's collectives and lax.ppermute only.
A program may use at most 64 MiB of HBM per device.

v0:
```python
import jax
import jax.numpy as jnp
from jax import lax
from jax.sharding import PartitionSpec as P


def step_math(summed, moment, second, weight, decay_rate):
    moment_next = 0.5 * moment + 0.5 * summed
    second_next = 0.5 * second + 0.5 * summed * summed
    update = moment_next / (jnp.sqrt(second_next) + 1e-06) + decay_rate * weight
    return (moment_next, second_next, update)


def on_device(
    grad_query,
    grad_output,
    grad_norm,
    grad_bias,
    weight_query,
    weight_output,
    weight_norm,
    weight_bias,
    first_query,
    first_output,
    first_norm,
    first_bias,
    second_query,
    second_output,
    second_norm,
    second_bias,
):
    weights = (weight_query, weight_output, weight_norm, weight_bias)
    moments = (first_query, first_output, first_norm, first_bias)
    seconds = (second_query, second_output, second_norm, second_bias)
    decay_rates = (0.01, 0.01, 0.0, 0.0)
    gradients = (grad_query[0], grad_output[0], grad_norm[0], grad_bias[0])
    totals = lax.psum(
        (gradients[0], gradients[1], gradients[2], gradients[3]), ("replica", "shard")
    )
    position = lax.axis_index("shard")
    summed_all = tuple(
        (
            lax.dynamic_slice_in_dim(entire, position * weight.shape[0], weight.shape[0], 0)
            for entire, weight in zip(totals, weights)
        )
    )
    results = [
        step_math(
            summed_all[member],
            moments[member],
            seconds[member],
            weights[member],
            decay_rates[member],
        )
        for member in range(4)
    ]
    weight_squares = [jnp.sum(weight * weight) for weight in weights]
    update_squares = [jnp.sum(result[2] * result[2]) for result in results]
    couples = [
        lax.psum((weight_squares[member], update_squares[member]), "shard") for member in range(4)
    ]
    weight_sizes = jnp.sqrt(jnp.stack([couple[0] for couple in couples]))
    update_sizes = jnp.sqrt(jnp.stack([couple[1] for couple in couples]))
    trust_ratios = weight_sizes / (update_sizes + 1e-06)
    shards = tuple(
        (
            (weights[member] - 0.01 * trust_ratios[member] * results[member][2]).astype(
                jnp.bfloat16
            )
            for member in range(4)
        )
    )
    gathered = (
        lax.all_gather(shards[0], "shard", axis=0, tiled=True),
        lax.all_gather(shards[1], "shard", axis=0, tiled=True),
        lax.all_gather(shards[2], "shard", axis=0, tiled=True),
        lax.all_gather(shards[3], "shard", axis=0, tiled=True),
    )
    norm_table = jnp.stack([weight_sizes, update_sizes])
    return (
        gathered[0],
        gathered[1],
        gathered[2],
        gathered[3],
        results[0][0],
        results[1][0],
        results[2][0],
        results[3][0],
        results[0][1],
        results[1][1],
        results[2][1],
        results[3][1],
        norm_table,
        trust_ratios,
    )


def solution(mesh):
    placed = (
        P(("replica", "shard"), None, None),
        P(("replica", "shard"), None, None),
        P(("replica", "shard"), None),
        P(("replica", "shard"), None, None),
        P("shard", None),
        P("shard", None),
        P("shard"),
        P("shard", None),
        P("shard", None),
        P("shard", None),
        P("shard"),
        P("shard", None),
        P("shard", None),
        P("shard", None),
        P("shard"),
        P("shard", None),
    )
    return jax.shard_map(
        on_device,
        mesh=mesh,
        in_specs=placed,
        out_specs=(
            P(),
            P(),
            P(),
            P(),
            P("shard", None),
            P("shard", None),
            P("shard"),
            P("shard", None),
            P("shard", None),
            P("shard", None),
            P("shard"),
            P("shard", None),
            P(),
            P(),
        ),
        check_vma=False,
    )
```

profile of v0, /device:TPU:1, one launch (start us, length us, event | category | flops | bytes accessed | tf_op | source)
XLA Modules:
  0.0 580.5 jit_solution(12802664677548248440)
XLA Ops:
  7.3 0.6 all-reduce.6.cloned.1.call-update
  7.9 0.1 copy.32
  8.0 1.3 dynamic-slice
  10.0 111.8 %all-reduce.1 = (f32[32,6]{1,0:T(8,128)S(1)}, f32[512]{0:T(512)S(1)}) all-reduce(f32[32,6]{1,0:T(8,128)S(1)} %bitcast.30, f32[512]{0:T(512)S(1)} %bitcast.32), channel_id=1, replica_groups=mesh['replica'=64,'shard'=8] {'replica','shard'}, use_global_device_ids=true, to_apply=%region_17.0 | all-reduce | flops 704 | bytes 5632 | tf_op jit(solution)/shard_map/psum | solution.py:37
  121.8 1.2 multiply_reduce_fusion.6
  123.0 1.2 multiply_reduce_fusion.4
  124.2 366.8 %all-reduce.6.cloned.1.call-done = (f32[384,512]{1,0:T(8,128)}, f32[512,384]{1,0:T(8,128)}) async-done(((f32[384,512]{1,0:T(8,128)}, f32[512,384]{1,0:T(8,128)}), (f32[384,512]{1,0:T(8,128)}, f32[512,384]{1,0:T(8,128)})) %all-reduce.6.cloned.1.call-update) | async-done | bytes 1572880 | tf_op jit(solution)/shard_map/psum | solution.py:37
  491.0 1.7 multiply_reduce_fusion.1
  492.7 1.6 multiply_reduce_fusion
  494.4 14.6 %all-reduce.3 = (f32[]{:T(128)}, f32[]{:T(128)}, f32[]{:T(128)}, f32[]{:T(128)}, f32[]{:T(128)}, /*index=5*/f32[]{:T(128)}, f32[]{:T(128)}, f32[]{:T(128)}) all-reduce(f32[]{:T(128)} %get-tuple-element.70, f32[]{:T(128)} %get-tuple-element.75, f32[]{:T(128)} %get-tuple-element.45, ...), channel_id=1, replica_groups=mesh['replica'=64,'shard'=8] {'shard'}, use_global_device_ids=true, to_apply=%region_7.0 | all-reduce | flops 8 | bytes 64 | tf_op jit(solution)/shard_map/psum | solution.py:60
  508.9 5.1 fusion.5
  514.1 0.6 fusion.11
  515.3 0.1 subtract_convert_fusion.1
  515.4 14.0 %all_gather.12 = bf16[512,384]{1,0:T(8,128)(2,1)S(1)} all-gather(bf16[64,384]{1,0:T(8,128)(2,1)S(1)} %subtract_convert_fusion.1), channel_id=1, replica_groups=mesh['replica'=64,'shard'=8] {'shard'}, dimensions={0}, use_global_device_ids=true | all-gather | bytes 442368 | tf_op jit(solution)/shard_map/all_gather | solution.py:74
  530.0 0.1 subtract_convert_fusion
  530.1 13.0 %all_gather.13 = bf16[384,512]{1,0:T(8,128)(2,1)S(1)} all-gather(bf16[48,512]{1,0:T(8,128)(2,1)S(1)} %subtract_convert_fusion), channel_id=1, replica_groups=mesh['replica'=64,'shard'=8] {'shard'}, dimensions={0}, use_global_device_ids=true | all-gather | bytes 442368 | tf_op jit(solution)/shard_map/all_gather | solution.py:75
  543.7 0.2 dynamic-update-slice
  544.0 12.5 %all-reduce = bf16[512]{0:T(512)(128)(2,1)} all-reduce(bf16[512]{0:T(512)(128)(2,1)S(1)} %dynamic-update-slice), channel_id=1, replica_groups=mesh['replica'=64,'shard'=8] {'shard'}, use_global_device_ids=true, to_apply=%add | all-reduce | flops 512 | bytes 2048
  557.1 8.6 %all-gather = bf16[8,4,6]{2,1,0:T(4,128)(2,1)S(1)} all-gather(bf16[1,4,6]{2,1,0:T(4,128)(2,1)S(1)} %fusion.3), channel_id=1, replica_groups=mesh['replica'=64,'shard'=8] {'shard'}, dimensions={0}, use_global_device_ids=true | all-gather | bytes 432 | tf_op jit(solution)/shard_map/all_gather | solution.py:77
  565.7 0.7 copy.33
  566.4 5.1 maximum_sqrt_fusion.2
  571.5 0.6 pad_maximum_fusion
  572.1 0.7 copy.41
  572.9 0.7 copy.42
  (42 shorter events, 0.1 us)
Async XLA Ops:
  7.2 483.8 %all-reduce.6.cloned.1.call-start = ((), (), s32[]{:S(2)}) async-start(), calls=%async_computation | async-start | bytes 3145728 | tf_op jit(solution)/shard_map/psum | solution.py:37
  7.2 0.7 copy-start.12
  7.2 2.7 copy-start.13
  7.2 114.5 %copy-start.14 = (f32[64]{0:T(128)S(1)}, f32[64]{0:T(128)}, u32[]{:S(2)}) copy-start(f32[64]{0:T(128)} %param.22) | copy-start | bytes 772
  7.3 114.5 %copy-start.17 = (f32[64]{0:T(128)S(1)}, f32[64]{0:T(128)}, u32[]{:S(2)}) copy-start(f32[64]{0:T(128)} %param.30) | copy-start | bytes 772
  7.3 114.5 %copy-start.18 = (f32[64]{0:T(128)S(1)}, f32[64]{0:T(128)}, u32[]{:S(2)}) copy-start(f32[64]{0:T(128)} %param.26) | copy-start | bytes 772
  7.3 115.7 %copy-start.11 = (f32[4,6]{1,0:T(4,128)S(1)}, f32[4,6]{1,0:T(4,128)}, u32[]{:S(2)}) copy-start(f32[4,6]{1,0:T(4,128)} %param.23) | copy-start | bytes 292
  7.3 115.7 %copy-start.15 = (f32[4,6]{1,0:T(4,128)S(1)}, f32[4,6]{1,0:T(4,128)}, u32[]{:S(2)}) copy-start(f32[4,6]{1,0:T(4,128)} %param.31) | copy-start | bytes 292
  7.3 115.7 %copy-start.16 = (f32[4,6]{1,0:T(4,128)S(1)}, f32[4,6]{1,0:T(4,128)}, u32[]{:S(2)}) copy-start(f32[4,6]{1,0:T(4,128)} %param.27) | copy-start | bytes 292
  7.3 483.6 %copy-start.6 = (f32[64,384]{1,0:T(8,128)S(1)}, f32[64,384]{1,0:T(8,128)}, u32[]{:S(2)}) copy-start(f32[64,384]{1,0:T(8,128)} %param.28) | copy-start | bytes 294916
  7.3 483.6 %copy-start.7 = (f32[64,384]{1,0:T(8,128)S(1)}, f32[64,384]{1,0:T(8,128)}, u32[]{:S(2)}) copy-start(f32[64,384]{1,0:T(8,128)} %param.24) | copy-start | bytes 294916
  7.9 483.0 %copy-start = (f32[64,384]{1,0:T(8,128)S(1)}, f32[64,384]{1,0:T(8,128)}, u32[]{:S(2)}) copy-start(f32[64,384]{1,0:T(8,128)} %param.20) | copy-start | bytes 294916
  491.0 1.7 copy-start.1
  491.0 1.7 copy-start.8
  491.0 1.7 copy-start.9
  492.7 22.6 %copy-start.2 = (f32[64,384]{1,0:T(8,128)}, f32[64,384]{1,0:T(8,128)S(1)}, u32[]{:S(2)}) copy-start(f32[64,384]{1,0:T(8,128)S(1)} %get-tuple-element.100) | copy-start | bytes 294916
  492.7 22.6 %copy-start.3 = (f32[64,384]{1,0:T(8,128)}, f32[64,384]{1,0:T(8,128)S(1)}, u32[]{:S(2)}) copy-start(f32[64,384]{1,0:T(8,128)S(1)} %get-tuple-element.96) | copy-start | bytes 294916
  494.4 35.6 %copy-start.4 = (f32[48,512]{1,0:T(8,128)}, f32[48,512]{1,0:T(8,128)S(1)}, u32[]{:S(2)}) copy-start(f32[48,512]{1,0:T(8,128)S(1)} %get-tuple-element.101) | copy-start | bytes 294916
  494.4 35.6 %copy-start.5 = (f32[48,512]{1,0:T(8,128)}, f32[48,512]{1,0:T(8,128)S(1)}, u32[]{:S(2)}) copy-start(f32[48,512]{1,0:T(8,128)S(1)} %get-tuple-element.97) | copy-start | bytes 294916
  514.1 0.6 copy-start.10
Sparse Core Ops, SparseCore 0:
  13.4 477.5 all-reduce.5
where the time goes:
time: 581 us; the launch traced here: 580 us
  waiting for transfers between devices  367 us (63%)
  blocking collectives  174 us (30%)
  between operations  17.4 us (3%)
  other arithmetic  16.7 us (3%)
    psum x1, waiting for transfers between devices, on_device(): lax.psum((gradients[0], gradients[1], gradients[2], gradients[3]), ('repl...  367 us
    psum x1, blocking collectives, on_device(): lax.psum((gradients[0], gradients[1], gradients[2], gradients[3]), ('repl...  112 us
    psum x1, blocking collectives, on_device(): lax.psum((weight_squares[member], update_squares[member]), 'shard')  14.6 us
    all_gather x1, blocking collectives, on_device(): lax.all_gather(shards[0], 'shard', axis=0, tiled=True)  14 us
    all_gather x1, blocking collectives, on_device(): lax.all_gather(shards[1], 'shard', axis=0, tiled=True)  13 us
    unnamed x1, blocking collectives  12.5 us
  transfers between devices with their start and end apart: 1, of which 1 were waited for; matrix products, arithmetic and copies ran while one was open for 1% of the time, Pallas kernels for 0%

commit v1 on v0

--- a/solution.py
+++ b/solution.py
@@ -35,7 +35,7 @@
     decay_rates = (0.01, 0.01, 0.0, 0.0)
     gradients = (grad_query[0], grad_output[0], grad_norm[0], grad_bias[0])
     totals = lax.psum(
-        (gradients[0], gradients[1], gradients[2], gradients[3]), ("replica", "shard")
+        lax.psum((gradients[0], gradients[1], gradients[2], gradients[3]), "shard"), "replica"
     )
     position = lax.axis_index("shard")
     summed_all = tuple(

time: 581 us -> 494 us (0.85)
  waiting for transfers between devices: 367 us -> 104 us
  blocking collectives: 174 us -> 350 us
    psum x1 -> x2, waiting for transfers between devices: 367 us -> 103 us  [the longest x1 85.8 us: on_device(): lax.psum((gradients[0], gradients[1], gradients[2], gradients[3]), 'shard')]
    psum x1 -> x2, blocking collectives: 112 us -> 249 us  [the longest x1 225 us: on_device(): lax.psum(lax.psum((gradients[0], gradients[1], gradients[2], gradients[3]...]
    psum x1, blocking collectives: 14.6 us -> 53.2 us  [on_device(): lax.psum((weight_squares[member], update_squares[member]), 'shard')]
  transfers between devices with their start and end apart: 1 -> 2, of which waited for: 1 -> 2; matrix products, arithmetic and copies ran while one was open for 1% -> 1% of each run, Pallas kernels for 0% -> 0%
where the time goes in v1:
time: 494 us
  blocking collectives  350 us (71%)
  waiting for transfers between devices  104 us (21%)
  between operations  17.4 us (4%)
  other arithmetic  16.7 us (3%)
  local copies, waits for them, and re-layouts  5.7 us (1%)
    psum x1, blocking collectives, on_device(): lax.psum(lax.psum((gradients[0], gradients[1], gradients[2], gradients[3]...  225 us
    psum x1, waiting for transfers between devices, on_device(): lax.psum((gradients[0], gradients[1], gradients[2], gradients[3]), 'shard')  85.8 us
    psum x1, blocking collectives, on_device(): lax.psum((weight_squares[member], update_squares[member]), 'shard')  53.2 us
    psum x1, blocking collectives, on_device(): lax.psum((gradients[0], gradients[1], gradients[2], gradients[3]), 'shard')  23.8 us
    psum x1, waiting for transfers between devices, on_device(): lax.psum(lax.psum((gradients[0], gradients[1], gradients[2], gradients[3]...  17.6 us
    all_gather x1, blocking collectives, on_device(): lax.all_gather(shards[0], 'shard', axis=0, tiled=True)  13.5 us
    all_gather x1, blocking collectives, on_device(): lax.all_gather(shards[1], 'shard', axis=0, tiled=True)  13 us
    unnamed x1, blocking collectives  12.5 us
  transfers between devices with their start and end apart: 2, of which 2 were waited for; matrix products, arithmetic and copies ran while one was open for 1% of the time, Pallas kernels for 0%

profile of v1, /device:TPU:1, one launch (start us, length us, event | category | flops | bytes accessed | tf_op | source)
XLA Modules:
  0.0 493.7 jit_solution(9678541555280084019)
XLA Ops:
  7.2 0.7 all-reduce.11.cloned.1.call-update
  8.0 85.8 %all-reduce.11.cloned.1.call-done = (f32[384,512]{1,0:T(8,128)}, f32[512,384]{1,0:T(8,128)}) async-done(((f32[384,512]{1,0:T(8,128)}, f32[512,384]{1,0:T(8,128)}), (f32[384,512]{1,0:T(8,128)}, f32[512,384]{1,0:T(8,128)})) %all-reduce.11.cloned.1.call-update) | async-done | bytes 1572880 | tf_op jit(solution)/shard_map/psum | solution.py:38
  93.8 0.6 copy-done.12
  94.5 1.3 dynamic-slice
  96.5 23.8 %all-reduce.4 = (f32[32,6]{1,0:T(8,128)S(1)}, f32[512]{0:T(512)S(1)}) all-reduce(f32[32,6]{1,0:T(8,128)S(1)} %bitcast.30, f32[512]{0:T(512)S(1)} %bitcast.32), channel_id=1, replica_groups=mesh['replica'=64,'shard'=8] {'shard'}, use_global_device_ids=true, to_apply=%region_20.0 | all-reduce | flops 704 | bytes 5632 | tf_op jit(solution)/shard_map/psum | solution.py:38
  120.3 225.2 %all-reduce.1 = (f32[32,6]{1,0:T(8,128)S(1)}, f32[512]{0:T(512)S(1)}) all-reduce(f32[32,6]{1,0:T(8,128)S(1)} %get-tuple-element.58, f32[512]{0:T(512)S(1)} %get-tuple-element.59), channel_id=1, replica_groups=mesh['replica'=64,'shard'=8] {'replica'}, use_global_device_ids=true, to_apply=%region_21.0 | all-reduce | flops 704 | bytes 5632 | tf_op jit(solution)/shard_map/psum | solution.py:37
  345.4 0.6 copy-done.14
  346.1 1.2 multiply_reduce_fusion.6
  347.3 1.2 multiply_reduce_fusion.4
  348.5 17.6 %all-reduce.9.cloned.1.call-done = (f32[384,512]{1,0:T(8,128)}, f32[512,384]{1,0:T(8,128)}) async-done(((f32[384,512]{1,0:T(8,128)}, f32[512,384]{1,0:T(8,128)}), (f32[384,512]{1,0:T(8,128)}, f32[512,384]{1,0:T(8,128)})) %all-reduce.9.cloned.1.call-update) | async-done | bytes 1572880 | tf_op jit(solution)/shard_map/psum | solution.py:37
  366.1 1.7 multiply_reduce_fusion.1
  367.8 1.6 multiply_reduce_fusion
  369.5 53.2 %all-reduce.3 = (f32[]{:T(128)}, f32[]{:T(128)}, f32[]{:T(128)}, f32[]{:T(128)}, f32[]{:T(128)}, /*index=5*/f32[]{:T(128)}, f32[]{:T(128)}, f32[]{:T(128)}) all-reduce(f32[]{:T(128)} %get-tuple-element.74, f32[]{:T(128)} %get-tuple-element.79, f32[]{:T(128)} %get-tuple-element.45, ...), channel_id=1, replica_groups=mesh['replica'=64,'shard'=8] {'shard'}, use_global_device_ids=true, to_apply=%region_7.0 | all-reduce | flops 8 | bytes 64 | tf_op jit(solution)/shard_map/psum | solution.py:60
  422.7 5.1 %fusion.5 = f32[4]{0:T(128)S(1)} fusion(f32[1]{0:T(128)} %bitcast.3, f32[1]{0:T(128)} %bitcast.2, f32[1]{0:T(128)} %bitcast.1, f32[1]{0:T(128)} %bitcast, f32[1]{0:T(128)} %bitcast.11, f32[1]{0:T(128)} %bitcast.9, f32[1]{0:T(128)} %bitcast.7, f32[1]{0:T(128)} %bitcast.5), kind=kLoop, calls=%fused_computation.27 | loop fusion | flops 32 | bytes 48 | tf_op jit(solution)/shard_map/div | solution.py:64
  427.9 0.6 fusion.11
  429.1 13.5 %all_gather.12 = bf16[512,384]{1,0:T(8,128)(2,1)S(1)} all-gather(bf16[64,384]{1,0:T(8,128)(2,1)S(1)} %subtract_convert_fusion.1), channel_id=1, replica_groups=mesh['replica'=64,'shard'=8] {'shard'}, dimensions={0}, use_global_device_ids=true | all-gather | bytes 442368 | tf_op jit(solution)/shard_map/all_gather | solution.py:74
  443.3 13.0 %all_gather.13 = bf16[384,512]{1,0:T(8,128)(2,1)S(1)} all-gather(bf16[48,512]{1,0:T(8,128)(2,1)S(1)} %subtract_convert_fusion), channel_id=1, replica_groups=mesh['replica'=64,'shard'=8] {'shard'}, dimensions={0}, use_global_device_ids=true | all-gather | bytes 442368 | tf_op jit(solution)/shard_map/all_gather | solution.py:75
  457.2 12.5 %all-reduce = bf16[512]{0:T(512)(128)(2,1)} all-reduce(bf16[512]{0:T(512)(128)(2,1)S(1)} %dynamic-update-slice), channel_id=1, replica_groups=mesh['replica'=64,'shard'=8] {'shard'}, use_global_device_ids=true, to_apply=%add | all-reduce | flops 512 | bytes 2048
  470.3 8.6 %all-gather = bf16[8,4,6]{2,1,0:T(4,128)(2,1)S(1)} all-gather(bf16[1,4,6]{2,1,0:T(4,128)(2,1)S(1)} %fusion.3), channel_id=1, replica_groups=mesh['replica'=64,'shard'=8] {'shard'}, dimensions={0}, use_global_device_ids=true | all-gather | bytes 432 | tf_op jit(solution)/shard_map/all_gather | solution.py:77
  479.0 0.7 copy.33
  479.6 5.1 %maximum_sqrt_fusion.2 = (f32[1,4]{1,0:T(1,128)S(1)}, f32[1,4]{1,0:T(1,128)S(1)}) fusion(f32[1,1]{1,0:T(1,128)} %bitcast.22, f32[1,1]{1,0:T(1,128)} %bitcast.21, f32[1,1]{1,0:T(1,128)} %bitcast.20, f32[1,1]{1,0:T(1,128)} %bitcast.19, f32[1,1]{1,0:T(1,128)} %bitcast.26, f32[1,1]{1,0:T(1,128)} %bitcast.25, f32[1,1]{1,0:T(1,128)} %bitcast.24, f32[1,1]{1,0:T(1,128)} %bitcast.23), kind=kLoop, calls=%fused_computation.30 | loop fusion | flops 24 | bytes 64 | tf_op jit(solution)/shard_map/sqrt | solution.py:62
  484.8 0.6 pad_maximum_fusion
  485.3 0.7 copy.43
  486.1 0.7 copy.44
  (46 shorter events, 0.6 us)
Async XLA Ops:
  7.2 86.5 %all-reduce.11.cloned.1.call-start = ((), (), s32[]{:S(2)}) async-start(), calls=%async_computation.1 | async-start | bytes 3145728 | tf_op jit(solution)/shard_map/psum | solution.py:38
  7.9 358.1 %all-reduce.9.cloned.1.call-start = ((), (), s32[]{:S(2)}) async-start(), calls=%async_computation | async-start | bytes 3145728 | tf_op jit(solution)/shard_map/psum | solution.py:37
  93.7 0.7 copy-start.12
  93.7 2.7 copy-start.13
  93.7 251.7 %copy-start.17 = (f32[64]{0:T(128)S(1)}, f32[64]{0:T(128)}, u32[]{:S(2)}) copy-start(f32[64]{0:T(128)} %param.30) | copy-start | bytes 772
  93.7 251.7 %copy-start.18 = (f32[64]{0:T(128)S(1)}, f32[64]{0:T(128)}, u32[]{:S(2)}) copy-start(f32[64]{0:T(128)} %param.26) | copy-start | bytes 772
  93.7 272.3 %copy-start.6 = (f32[64,384]{1,0:T(8,128)S(1)}, f32[64,384]{1,0:T(8,128)}, u32[]{:S(2)}) copy-start(f32[64,384]{1,0:T(8,128)} %param.28) | copy-start | bytes 294916
  93.7 272.3 %copy-start.7 = (f32[64,384]{1,0:T(8,128)S(1)}, f32[64,384]{1,0:T(8,128)}, u32[]{:S(2)}) copy-start(f32[64,384]{1,0:T(8,128)} %param.24) | copy-start | bytes 294916
  93.8 272.3 %copy-start = (f32[64,384]{1,0:T(8,128)S(1)}, f32[64,384]{1,0:T(8,128)}, u32[]{:S(2)}) copy-start(f32[64,384]{1,0:T(8,128)} %param.20) | copy-start | bytes 294916
  96.4 250.8 %copy-start.11 = (f32[4,6]{1,0:T(4,128)S(1)}, f32[4,6]{1,0:T(4,128)}, u32[]{:S(2)}) copy-start(f32[4,6]{1,0:T(4,128)} %param.23) | copy-start | bytes 292
  96.4 250.8 %copy-start.15 = (f32[4,6]{1,0:T(4,128)S(1)}, f32[4,6]{1,0:T(4,128)}, u32[]{:S(2)}) copy-start(f32[4,6]{1,0:T(4,128)} %param.31) | copy-start | bytes 292
  96.5 250.8 %copy-start.16 = (f32[4,6]{1,0:T(4,128)S(1)}, f32[4,6]{1,0:T(4,128)}, u32[]{:S(2)}) copy-start(f32[4,6]{1,0:T(4,128)} %param.27) | copy-start | bytes 292
  345.4 0.7 copy-start.14
  366.1 1.8 copy-start.1
  366.1 1.7 copy-start.8
  366.1 1.7 copy-start.9
  367.8 61.2 %copy-start.2 = (f32[64,384]{1,0:T(8,128)}, f32[64,384]{1,0:T(8,128)S(1)}, u32[]{:S(2)}) copy-start(f32[64,384]{1,0:T(8,128)S(1)} %get-tuple-element.104) | copy-start | bytes 294916
  367.8 61.2 %copy-start.3 = (f32[64,384]{1,0:T(8,128)}, f32[64,384]{1,0:T(8,128)S(1)}, u32[]{:S(2)}) copy-start(f32[64,384]{1,0:T(8,128)S(1)} %get-tuple-element.100) | copy-start | bytes 294916
  369.5 73.7 %copy-start.4 = (f32[48,512]{1,0:T(8,128)}, f32[48,512]{1,0:T(8,128)S(1)}, u32[]{:S(2)}) copy-start(f32[48,512]{1,0:T(8,128)S(1)} %get-tuple-element.105) | copy-start | bytes 294916
  369.5 73.7 %copy-start.5 = (f32[48,512]{1,0:T(8,128)}, f32[48,512]{1,0:T(8,128)S(1)}, u32[]{:S(2)}) copy-start(f32[48,512]{1,0:T(8,128)S(1)} %get-tuple-element.101) | copy-start | bytes 294916
  427.8 0.6 copy-start.10
Sparse Core Ops, SparseCore 0:
  10.5 83.2 all-reduce.10
  97.2 268.8 all-reduce.8
